TPU v7x, 32 devices: a whole 2x2x4 slice. The times are simulated.
32 devices in a mesh: ctx: 4 (over y, x), dp: 4 (over z), tp: 2 (over core).
Axes of the slice: x: 2, y: 2, z: 4, core: 2. Of those that a mesh axis runs over, the one named last changes fastest.
Arguments:
- queries: bfloat16 [4, 512, 32, 128], P('dp', 'ctx', 'tp'), may hold values from -21 to 21
- keys: bfloat16 [4, 512, 4, 128], P('dp', 'ctx', 'tp'), may hold values from -6 to 6
- values: bfloat16 [4, 512, 4, 128], P('dp', 'ctx', 'tp'), may hold values from -6 to 6
- output_cotangent: bfloat16 [4, 512, 32, 128], P('dp', 'ctx', 'tp'), may hold values from -6 to 6
- features: bfloat16 [4, 512, 4096], P('dp', 'ctx'), may hold values from -60 to 60
- doc_lengths: int32 [4, 48], P('dp'), may hold values from 1 to 16, 512 in all within a row
- rope_num: int32 [64], replicated, may hold values from 1 to 40
- rope_den: int32 [64], replicated, may hold values from 1 to 8
- param: float32 [4096, 512], P('dp', 'tp'), may hold values from -0.4375 to 0.4375
- first_moment_state: float32 [4096, 512], P('dp', 'tp'), may hold values from -4 to 4
- second_moment_state: float32 [4096, 512], P('dp', 'tp'), may hold values from 0.05 to 1
Outputs:
- grad_queries: bfloat16 [4, 512, 32, 128], P('dp', 'ctx', 'tp')
- grad_keys: bfloat16 [4, 512, 4, 128], P('dp', 'ctx', 'tp')
- value_gradient: bfloat16 [4, 512, 4, 128], P('dp', 'ctx', 'tp')
- new_param: float32 [4096, 512], P('dp', 'tp')
- new_first: float32 [4096, 512], P('dp', 'tp')
- new_second: float32 [4096, 512], P('dp', 'tp')
Inputs may be any that keep to these rules, and one draw needn't show every extreme that they name: `doc_lengths`: each row's 48 lengths sum to 512, and the largest of each row is exactly 16.
All inputs are finite; a program needn't handle non-finite values.
Results may differ from a plain program's by a relative error of at most 0.0064.
Values may be sent and summed in bfloat16 or wider, within the bound.
No kernel may reach another device: no remote copies, remote signals or barrier semaphores. Data moves between devices by JAX's collectives and lax.ppermute only.
A program may use at most 64 MiB of HBM per device.

v0:
```python
from functools import reduce
import math
import jax
import jax.numpy as jnp
from jax import lax
from jax.sharding import PartitionSpec as P

ROPE_BASE = 500000.0
NEG_FILL = -1e30
CLIP_NORM = 1000.0
LEARN_RATE = 0.0001
DECAY_RATE = 0.1
BETA_ONE = 0.9
BETA_TWO = 0.95
ADAM_EPS = 1e-08
FIRST_FIX = 1.0 - 0.9**10
SECOND_FIX = 1.0 - 0.95**10


def shifted(array, axis, by):
    peers = lax.axis_size(axis)
    pairs = [(i, i + by) for i in range(peers) if 0 <= i + by < peers]
    return lax.ppermute(array, axis, pairs)


def doc_layout(lengths_row, token_index):
    doc_ends = jnp.cumsum(lengths_row)
    passed = doc_ends[None, :] <= token_index[:, None]
    doc_start = jnp.max(jnp.where(passed, doc_ends[None, :], 0), axis=1)
    doc_id = jnp.sum(passed.astype(jnp.int32), axis=1)
    return (doc_id, (token_index - doc_start).astype(jnp.float32))


def rope_tables(position, rope_num, rope_den, head_dim):
    expo = jnp.arange(head_dim // 2, dtype=jnp.float32) * (2.0 / head_dim)
    freq = (
        jnp.exp(-math.log(ROPE_BASE) * expo)
        * rope_den.astype(jnp.float32)
        / rope_num.astype(jnp.float32)
    )
    angle = position[:, None] * freq[None, :]
    cosine = jnp.concatenate([jnp.cos(angle), jnp.cos(angle)], axis=1)
    sine = jnp.concatenate([jnp.sin(angle), jnp.sin(angle)], axis=1)
    return (cosine[:, None, :], sine[:, None, :])


def rotate(vectors, cosine, sine):
    half = vectors.shape[-1] // 2
    turned = jnp.concatenate([-vectors[..., half:], vectors[..., :half]], axis=-1)
    return vectors * cosine + turned * sine


def unrotate(grads_in, cosine, sine):
    half = grads_in.shape[-1] // 2
    scaled = grads_in * sine
    turned = jnp.concatenate([scaled[..., half:], -scaled[..., :half]], axis=-1)
    return grads_in * cosine + turned


def adam_update(param, first_moment_state, second_moment_state, weight_gradient, grad_total):
    clip_factor = jnp.minimum(jnp.float32(1.0), CLIP_NORM / jnp.sqrt(grad_total))
    clipped = weight_gradient * clip_factor
    new_first = BETA_ONE * first_moment_state + (1.0 - BETA_ONE) * clipped
    new_second = BETA_TWO * second_moment_state + (1.0 - BETA_TWO) * clipped * clipped
    step_size = new_first / FIRST_FIX / (jnp.sqrt(new_second / SECOND_FIX) + ADAM_EPS)
    new_param = param - LEARN_RATE * (step_size + DECAY_RATE * param)
    return (new_param, new_first, new_second)


def local(
    queries,
    keys,
    values,
    output_cotangent,
    features,
    doc_lengths,
    rope_num,
    rope_den,
    param,
    first_moment_state,
    second_moment_state,
):
    tok_rows = queries.shape[1]
    head_count = queries.shape[2]
    head_dim = queries.shape[3]
    kv_count = keys.shape[2]
    group_size = head_count // kv_count
    n_ctx = lax.axis_size("ctx")
    place = lax.axis_index("ctx")
    seq_len = tok_rows * n_ctx
    doc_most = seq_len // 32
    reach = (doc_most + tok_rows - 2) // tok_rows
    scale = head_dim ** (-0.5)
    lengths_row = doc_lengths[0]
    own_index = place * tok_rows + jnp.arange(tok_rows, dtype=jnp.int32)
    own_doc, position = doc_layout(lengths_row, own_index)
    cosine, sine = rope_tables(position, rope_num, rope_den, head_dim)
    rotated_query_rows = rotate(queries[0].astype(jnp.float32), cosine, sine).astype(jnp.bfloat16)
    rotated_query_rows = rotated_query_rows.reshape(tok_rows, kv_count, group_size, head_dim)
    rotated_key_rows = rotate(keys[0].astype(jnp.float32), cosine, sine).astype(jnp.bfloat16)
    grad_out = output_cotangent[0].reshape(tok_rows, kv_count, group_size, head_dim)
    kv_pair = jnp.stack([rotated_key_rows, values[0]])
    pairs = [kv_pair]
    offset = 1
    kv_pair = shifted(kv_pair, "ctx", 1)
    pairs.append(kv_pair)
    masks = []
    for offset in range(reach + 1):
        key_index = (place - offset) * tok_rows + jnp.arange(tok_rows, dtype=jnp.int32)
        key_doc = doc_layout(lengths_row, key_index)[0]
        valid = (
            (key_index[None, :] >= 0)
            & (key_index[None, :] <= own_index[:, None])
            & (key_doc[None, :] == own_doc[:, None])
        )
        masks.append(valid)
    score_list = []
    for pair_in, valid_in in zip(pairs, masks):
        raw = (
            jnp.einsum(
                "qhgd,khd->hgqk", rotated_query_rows, pair_in[0], preferred_element_type=jnp.float32
            )
            * scale
        )
        score_list.append(jnp.where(valid_in, raw, NEG_FILL))
    row_top = reduce(
        jnp.maximum, [jnp.max(scores, axis=-1, keepdims=True) for scores in score_list]
    )
    weight_list = [
        jnp.where(valid_in, jnp.exp(scores - row_top), 0.0)
        for scores, valid_in in zip(score_list, masks)
    ]
    row_total = reduce(
        jnp.add, [jnp.sum(weights, axis=-1, keepdims=True) for weights in weight_list]
    )
    prob_list = [weights / row_total for weights in weight_list]
    low_list = [probs.astype(jnp.bfloat16) for probs in prob_list]
    attn_out = reduce(
        jnp.add,
        [
            jnp.einsum("hgqk,khd->qhgd", probs_low, pair_in[1], preferred_element_type=jnp.float32)
            for probs_low, pair_in in zip(low_list, pairs)
        ],
    )
    delta = jnp.einsum("qhgd,qhgd->hgq", grad_out.astype(jnp.float32), attn_out)[..., None]
    query_terms = []
    key_terms = []
    for pair_in, probs, probs_low, valid_in in zip(pairs, prob_list, low_list, masks):
        dprobs = jnp.einsum(
            "qhgd,khd->hgqk", grad_out, pair_in[1], preferred_element_type=jnp.float32
        )
        dscores = (probs * (dprobs - delta)).astype(jnp.bfloat16)
        q_part = (
            jnp.einsum("hgqk,khd->qhgd", dscores, pair_in[0], preferred_element_type=jnp.float32)
            * scale
        )
        k_part = (
            jnp.einsum(
                "hgqk,qhgd->khd", dscores, rotated_query_rows, preferred_element_type=jnp.float32
            )
            * scale
        )
        v_part = jnp.einsum(
            "hgqk,qhgd->khd", probs_low, grad_out, preferred_element_type=jnp.float32
        )
        q_part, kv_part = (q_part, jnp.stack([k_part, v_part]))
        query_terms.append(q_part)
        key_terms.append(kv_part)
    query_grad = reduce(jnp.add, query_terms)
    key_total = key_terms[reach]
    offset = 0
    key_total = (
        shifted(key_total.astype(jnp.bfloat16), "ctx", -1).astype(key_total.dtype)
        + key_terms[offset]
    )
    grad_q = unrotate(query_grad.reshape(tok_rows, head_count, head_dim), cosine, sine).astype(
        jnp.bfloat16
    )
    grad_k = unrotate(key_total[0], cosine, sine).astype(jnp.bfloat16)
    grad_v = key_total[1].astype(jnp.bfloat16)
    feats = features[0]
    width = feats.shape[1]
    value_flat = grad_v.reshape(tok_rows, kv_count * head_dim)
    own_rows = param.shape[0]
    n_dp = lax.axis_size("dp")
    piece_rows = own_rows // n_ctx
    permuted = (
        feats.reshape(tok_rows, n_dp, n_ctx, piece_rows)
        .transpose(0, 2, 1, 3)
        .reshape(tok_rows, width)
    )
    pieces = lax.psum_scatter(
        lax.dot_general(
            permuted, value_flat, (((0,), (0,)), ((), ())), preferred_element_type=jnp.float32
        ),
        ("ctx", "dp"),
        scatter_dimension=0,
        tiled=True,
    )
    weight_gradient = lax.all_gather(pieces, "ctx", axis=0, tiled=True)
    norm_part = jnp.sum(weight_gradient * weight_gradient)
    grad_total = lax.psum(norm_part, ("dp", "tp"))
    new_param, new_first, new_second = adam_update(
        param, first_moment_state, second_moment_state, weight_gradient, grad_total
    )
    return (grad_q[None], grad_k[None], grad_v[None], new_param, new_first, new_second)


def solution(mesh):
    placed = (
        P("dp", "ctx", "tp", None),
        P("dp", "ctx", "tp", None),
        P("dp", "ctx", "tp", None),
        P("dp", "ctx", "tp", None),
        P("dp", "ctx", None),
        P("dp", None),
        P(),
        P(),
        P("dp", "tp"),
        P("dp", "tp"),
        P("dp", "tp"),
    )
    return jax.shard_map(
        local,
        mesh=mesh,
        in_specs=placed,
        out_specs=(
            P("dp", "ctx", "tp", None),
            P("dp", "ctx", "tp", None),
            P("dp", "ctx", "tp", None),
            P("dp", "tp"),
            P("dp", "tp"),
            P("dp", "tp"),
        ),
        check_vma=False,
    )
```

profile of v0, /device:TPU:0, one launch (start us, length us, event | category | flops | bytes accessed | tf_op | source)
XLA Modules:
  0.0 216.5 jit_solution(16039566260402643105)
XLA Ops:
  7.2 0.7 copy.135
  8.0 0.1 reduce.1
  8.2 0.1 fusion.44
  8.3 0.7 convert_divide_fusion
  9.0 0.3 multiply_cosine_fusion
  9.4 0.9 convert_bitcast_fusion.2
  10.3 0.7 fusion.45
  11.0 0.8 copy.142
  11.9 0.9 fusion.35
  12.8 0.7 pad_maximum_fusion
  13.5 5.5 %collective-permute-start = (bf16[2,128,2,128]{3,1,2,0:T(8,128)(2,1)}, bf16[2,128,2,128]{3,1,2,0:T(8,128)(2,1)}, u32[]{:S(2)}, u32[]{:S(2)}) collective-permute-start(bf16[2,128,2,128]{3,1,2,0:T(8,128)(2,1)} %pad_maximum_fusion), channel_id=1, source_target_pairs={{0,8},{8,16},{16,24},{1,9},{9,17},{17,25},{2,10},{10,18},{18,26},{... | collective-permute-start | bytes 393224 | tf_op jit(solution)/shard_map/ppermute | solution.py:23
  19.0 0.6 broadcast_compare_fusion
  19.7 0.7 copy.140
  20.4 1.2 convert_bitcast_fusion.1
  21.6 1.3 fusion.22
  22.9 2.4 %copy.138 = f32[128,2,8,64]{0,3,2,1:T(8,128)} copy(f32[128,2,8,64]{3,2,1,0:T(8,128)} %get-tuple-element.40) | data formatting | bytes 1048576 | tf_op jit(solution)/shard_map/concatenate | solution.py:49
  25.3 1.2 copy.139
  26.5 0.4 copy.137
  27.0 1.0 fusion.40
  28.0 0.8 compare_and_fusion
  28.8 1.4 fusion.24
  30.2 0.3 fusion.51
  30.5 1.2 copy.164
  31.8 1.6 copy.168
  33.4 1.0 copy.169
  34.4 1.1 fusion.52
  35.6 0.4 fusion.29
  36.0 1.0 fusion.18
  37.0 1.0 convolution_bitcast_fusion.5
  38.0 0.4 convolution_bitcast_fusion.3
  38.5 1.2 fusion.3
  39.7 0.8 multiply_reduce_fusion
  40.5 1.4 fusion.12
  42.0 1.6 fusion.11
  43.6 0.3 fusion.19
  43.9 1.3 collective-permute-start.1
  45.2 0.3 fusion.15
  45.6 5.2 %collective-permute-done.1 = bf16[2,128,2,128]{3,1,2,0:T(8,128)(2,1)S(1)} collective-permute-done((bf16[2,128,2,128]{3,1,2,0:T(8,128)(2,1)S(1)}, bf16[2,128,2,128]{3,1,2,0:T(8,128)(2,1)S(1)}, u32[]{:S(2)}, u32[]{:S(2)}) %collective-permute-start.1) | collective-permute-done | bytes 131104 | tf_op jit(solution)/shard_map/ppermute | solution.py:23
  50.9 0.1 copy.167
  51.0 0.5 copy-done.8
  51.5 2.6 %convolution_bitcast_fusion = f32[4096,256]{0,1:T(8,128)} fusion(bf16[128,256]{0,1:T(8,128)(2,1)S(1)} %bitcast.172, bf16[128,4096]{0,1:T(8,128)(2,1)S(1)} %bitcast.170), kind=kOutput, calls=%fused_computation | convolution fusion | flops 268435456 | bytes 5308416 | tf_op jit(solution)/shard_map/dot_general | solution.py:193
  54.2 0.2 all-gather.2.cloned.1.call-start
  54.4 1.0 copy-done.6
  55.4 1.3 copy.166
  56.7 1.3 copy.170
  58.0 2.5 %copy.172 = f32[1024,256]{0,1:T(8,128)} copy(f32[1024,256]{1,0:T(8,128)} %param.19) | data formatting | bytes 2097152 | tf_op args[8]
  60.5 1.2 fusion.53
  61.7 90.6 %reduce-scatter.2.cloned.1.call-done = f32[256,256]{0,1:T(8,128)} async-done(((f32[4096,256]{0,1:T(8,128)}), f32[256,256]{0,1:T(8,128)}) %reduce-scatter.2.cloned.1.call-update) | async-done | bytes 262160 | tf_op jit(solution)/shard_map/reduce_scatter | solution.py:192
  152.3 1.2 fusion.6
  153.5 0.5 copy.157
  154.0 0.5 copy.156
  154.5 0.1 broadcast_multiply_fusion
  154.7 0.3 slice_bitcast_fusion
  155.0 1.2 fusion.25
  156.2 0.7 copy.174
  157.0 0.1 fusion.39
  157.1 22.0 %all-gather.2.cloned.1.call-done = f32[1024,256]{0,1:T(8,128)} async-done(((f32[256,256]{0,1:T(8,128)}), f32[1024,256]{0,1:T(8,128)}) %all-gather.2.cloned.1.call-update) | async-done | bytes 1048592 | tf_op jit(solution)/shard_map/all_gather | solution.py:200
  179.1 2.2 %multiply_reduce_fusion.1 = f32[]{:T(128)} fusion(f32[1024,256]{0,1:T(8,128)} %all-gather.2.cloned.1.call-done), kind=kLoop, calls=%fused_computation.50 | loop fusion | flops 524287 | bytes 1048580 | tf_op jit(solution)/shard_map/reduce_sum | solution.py:201
  181.3 0.7 copy.173
  182.0 16.9 %psum.7 = f32[]{:T(128)} all-reduce(f32[]{:T(128)} %multiply_reduce_fusion.1), channel_id=1, replica_groups=mesh['ctx'=4,'dp'=4,'tp'=2] {'dp','tp'}, use_global_device_ids=true, to_apply=%region_10.11 | all-reduce | flops 1 | bytes 8 | tf_op jit(solution)/shard_map/psum | solution.py:202
  199.7 3.7 %multiply_subtract_fusion = (f32[1024,256]{0,1:T(8,128)}, f32[1024,256]{0,1:T(8,128)}, f32[1024,256]{0,1:T(8,128)S(1)}) fusion(f32[1024,256]{0,1:T(8,128)} %copy.172, f32[1024,256]{0,1:T(8,128)} %all-gather.2.cloned.1.call-done, f32[]{:T(128)S(6)} %min_shard_map.3, f32[1024,256]{0,1:T(8,128)S(1)} %copy-done.1, f32[1024,256]{0,1:T(8,128)S(1)} %copy-done.2), kind=kLoop, calls=%fused_computation.48 | loop fusion | flops 4194304 | bytes 7340036 | tf_op jit(solution)/shard_map/sub | solution.py:66
  203.3 2.5 %copy.175 = f32[1024,256]{1,0:T(8,128)} copy(f32[1024,256]{0,1:T(8,128)} %get-tuple-element.35) | data formatting | bytes 2097152
  205.9 2.5 %copy.176 = f32[1024,256]{1,0:T(8,128)} copy(f32[1024,256]{0,1:T(8,128)} %get-tuple-element.36) | data formatting | bytes 2097152
  208.4 1.3 copy.177
  (48 shorter events, 0.7 us)
Async XLA Ops:
  7.2 145.1 %reduce-scatter.2.cloned.1.call-start = ((), (), s32[]{:S(2)}) async-start(), calls=%async_computation.1 | async-start | bytes 4456448 | tf_op jit(solution)/shard_map/reduce_scatter | solution.py:192
  13.5 21.0 %collective-permute-start = (bf16[2,128,2,128]{3,1,2,0:T(8,128)(2,1)}, bf16[2,128,2,128]{3,1,2,0:T(8,128)(2,1)}, u32[]{:S(2)}, u32[]{:S(2)}) collective-permute-start(bf16[2,128,2,128]{3,1,2,0:T(8,128)(2,1)} %pad_maximum_fusion), channel_id=1, source_target_pairs={{0,8},{8,16},{16,24},{1,9},{9,17},{17,25},{2,10},{10,18},{18,26},{... | collective-permute-start | bytes 393224 | tf_op jit(solution)/shard_map/ppermute | solution.py:23
  21.6 5.4 %copy-start.11 = (bf16[1,128,2,128]{3,2,1,0:T(2,128)(2,1)S(1)}, bf16[1,128,2,128]{3,2,1,0:T(2,128)(2,1)}, u32[]{:S(2)}) copy-start(bf16[1,128,2,128]{3,2,1,0:T(2,128)(2,1)} %param.12) | copy-start | bytes 196612
  25.3 5.2 %copy-start.3 = (bf16[1,128,16,128]{3,2,1,0:T(8,128)(2,1)S(1)}, bf16[1,128,16,128]{3,2,1,0:T(8,128)(2,1)}, u32[]{:S(2)}) copy-start(bf16[1,128,16,128]{3,2,1,0:T(8,128)(2,1)} %param.14) | copy-start | bytes 1572868
  28.0 2.5 %copy-start.10 = (bf16[128,2,128,1]{2,0,3,1:T(8,128)(2,1)}, bf16[128,2,128,1]{2,0,3,1:T(8,128)(2,1)S(1)}, u32[]{:S(2)}) copy-start(bf16[128,2,128,1]{2,0,3,1:T(8,128)(2,1)S(1)} %fusion.40) | copy-start | bytes 196612
  33.4 2.6 %copy-start.12 = (bf16[128,2,8,128]{0,3,2,1:T(8,128)(2,1)S(1)}, bf16[128,2,8,128]{0,3,2,1:T(8,128)(2,1)}, u32[]{:S(2)}) copy-start(bf16[128,2,8,128]{0,3,2,1:T(8,128)(2,1)} %copy.164) | copy-start | bytes 1572868
  36.0 2.0 copy-start.14
  42.0 1.9 copy-start.15
  42.0 8.8 %copy-start.13 = (f32[1,128,2,128]{3,1,2,0:T(8,128)S(1)}, f32[1,128,2,128]{3,1,2,0:T(8,128)}, u32[]{:S(2)}) copy-start(f32[1,128,2,128]{3,1,2,0:T(8,128)} %convolution_bitcast_fusion.5) | copy-start | bytes 393220
  42.0 9.5 %copy-start = (bf16[128,4,4,256]{0,3,2,1:T(8,128)(2,1)S(1)}, bf16[128,4,4,256]{0,3,2,1:T(8,128)(2,1)}, u32[]{:S(2)}) copy-start(bf16[128,4,4,256]{0,3,2,1:T(8,128)(2,1)} %copy.169) | copy-start | bytes 3145732
  43.6 2.0 copy-start.4
  43.9 6.9 %collective-permute-start.1 = (bf16[2,128,2,128]{3,1,2,0:T(8,128)(2,1)S(1)}, bf16[2,128,2,128]{3,1,2,0:T(8,128)(2,1)S(1)}, u32[]{:S(2)}, u32[]{:S(2)}) collective-permute-start(bf16[2,128,2,128]{3,1,2,0:T(8,128)(2,1)S(1)} %pad_maximum_fusion.1), channel_id=1, source_target_pairs={{8,0},{16,8},{24,16},{9,1},{17,9},{25,17},{10,2},{18,10},{26,18},{... | collective-permute-start | bytes 393224 | tf_op jit(solution)/shard_map/ppermute | solution.py:23
  50.9 0.6 copy-start.8
  54.1 1.2 copy-start.6
  54.1 2.5 %copy-start.7 = (f32[1024,256]{1,0:T(8,128)S(1)}, f32[1024,256]{1,0:T(8,128)}, u32[]{:S(2)}) copy-start(f32[1024,256]{1,0:T(8,128)} %param.21) | copy-start | bytes 3145732
  54.2 98.2 %copy-start.5 = (bf16[2,8,128,128]{2,3,1,0:T(8,128)(2,1)S(1)}, bf16[2,8,128,128]{2,3,1,0:T(8,128)(2,1)}, u32[]{:S(2)}) copy-start(bf16[2,8,128,128]{2,3,1,0:T(8,128)(2,1)} %copy-done.4) | copy-start | bytes 1572868
  54.2 125.0 %all-gather.2.cloned.1.call-start = ((), (), s32[]{:S(2)}) async-start(), calls=%async_computation.2 | async-start | bytes 1310720 | tf_op jit(solution)/shard_map/all_gather | solution.py:200
  154.7 1.6 copy-start.9
  155.0 44.6 %copy-start.1 = (f32[1024,256]{0,1:T(8,128)S(1)}, f32[1024,256]{0,1:T(8,128)}, u32[]{:S(2)}) copy-start(f32[1024,256]{0,1:T(8,128)} %copy.166) | copy-start | bytes 3145732
  155.0 44.6 %copy-start.2 = (f32[1024,256]{0,1:T(8,128)S(1)}, f32[1024,256]{0,1:T(8,128)}, u32[]{:S(2)}) copy-start(f32[1024,256]{0,1:T(8,128)} %copy.170) | copy-start | bytes 3145732
Sparse Core Ops, SparseCore 0:
  54.3 97.9 reduce-scatter.1
  154.1 24.9 all-gather.1
where the time goes:
time: 218 us; the launch traced here: 217 us
  waiting for transfers between devices  118 us (54%)
  local copies, waits for them, and re-layouts  26 us (12%)
  other arithmetic  19.8 us (9%)
  blocking collectives  16.9 us (8%)
  between operations  15.2 us (7%)
  matrix products  13.7 us (6%)
  starting transfers between devices  7.07 us (3%)
    reduce_scatter x1, waiting for transfers between devices, local(): lax.psum_scatter(lax.dot_general(permuted, value_flat, (((0,), (0,)), (()...  90.6 us
    all_gather x1, waiting for transfers between devices, local(): weight_gradient = lax.all_gather(pieces, 'ctx', axis=0, tiled=True)  22 us
    unnamed x42, local copies, waits for them, and re-layouts  16.9 us
    psum x1, blocking collectives, local(): grad_total = lax.psum(norm_part, ('dp', 'tp'))  16.9 us
    ppermute x2, starting transfers between devices, shifted(): return lax.ppermute(array, axis, pairs)  6.81 us
    ppermute x2, waiting for transfers between devices, shifted(): return lax.ppermute(array, axis, pairs)  5.25 us
  transfers between devices with their start and end apart: 4, of which 3 were waited for; matrix products, arithmetic and copies ran while one was open for 12% of the time, Pallas kernels for 0%

commit v1 on v0

--- a/solution.py
+++ b/solution.py
@@ -4,6 +4,7 @@
 import jax.numpy as jnp
 from jax import lax
 from jax.sharding import PartitionSpec as P
+from jax.lax import axis_index, axis_size, ppermute
 
 ROPE_BASE = 500000.0
 NEG_FILL = -1e30
@@ -15,6 +16,20 @@
 ADAM_EPS = 1e-08
 FIRST_FIX = 1.0 - 0.9**10
 SECOND_FIX = 1.0 - 0.95**10
+
+
+def _bring_halves(vals, group_axis="ctx"):
+    n_blocks = axis_size(group_axis)
+    gallery = [(at, (at + 1) % n_blocks) for at in range(n_blocks)]
+    m_next, main = ([vals], [vals])
+    kept_rows = [(at, (at - 1) % n_blocks) for at in range(n_blocks)]
+    for _ in range(n_blocks // 2):
+        m_next.append(ppermute(m_next[-1], group_axis, gallery))
+    for _ in range((n_blocks - 1) // 2):
+        main.append(ppermute(main[-1], group_axis, kept_rows))
+    base_arr = jnp.concatenate([*m_next[::-1], *main[1:]], 0)
+    v_next = jnp.roll(base_arr, (axis_index(group_axis) - n_blocks // 2) * vals.shape[0], 0)
+    return v_next
 
 
 def shifted(array, axis, by):
@@ -197,7 +212,7 @@
         scatter_dimension=0,
         tiled=True,
     )
-    weight_gradient = lax.all_gather(pieces, "ctx", axis=0, tiled=True)
+    weight_gradient = _bring_halves(pieces)
     norm_part = jnp.sum(weight_gradient * weight_gradient)
     grad_total = lax.psum(norm_part, ("dp", "tp"))
     new_param, new_first, new_second = adam_update(

time: 218 us -> 201 us (0.922)
  waiting for transfers between devices: 118 us -> 107 us
  other arithmetic: 19.8 us -> 16.9 us
  starting transfers between devices: 7.07 us -> 9.96 us
  blocking collectives: 16.9 us -> 14.3 us
    all_gather x1 -> x0, waiting for transfers between devices: 22 us -> none  [local(): weight_gradient = lax.all_gather(pieces, 'ctx', axis=0, tiled=True)]
    ppermute x0 -> x3, waiting for transfers between devices: none -> 12.7 us  [the longest x2 10.8 us: _bring_halves(): m_next.append(ppermute(m_next[-1], group_axis, gallery))]
    ppermute x0 -> x3, starting transfers between devices: none -> 2.98 us  [the longest x1 2.97 us: _bring_halves(): main.append(ppermute(main[-1], group_axis, kept_rows))]
    psum x1, blocking collectives: 16.9 us -> 14.3 us  [local(): grad_total = lax.psum(norm_part, ('dp', 'tp'))]
    unnamed x42 -> x65, local copies, waits for them, and re-layouts: 16.9 us -> 17.1 us
  transfers between devices with their start and end apart: 4 -> 6, of which waited for: 3 -> 5; matrix products, arithmetic and copies ran while one was open for 12% -> 11% of each run, Pallas kernels for 0% -> 0%
where the time goes in v1:
time: 201 us; the launch traced here: 200 us
  waiting for transfers between devices  107 us (53%)
  local copies, waits for them, and re-layouts  24.7 us (12%)
  other arithmetic  16.9 us (8%)
  between operations  15.4 us (8%)
  blocking collectives  14.3 us (7%)
  matrix products  12.7 us (6%)
  starting transfers between devices  9.96 us (5%)
    reduce_scatter x1, waiting for transfers between devices, local(): lax.psum_scatter(lax.dot_general(permuted, value_flat, (((0,), (0,)), (()...  88.6 us
    unnamed x65, local copies, waits for them, and re-layouts  17.1 us
    psum x1, blocking collectives, local(): grad_total = lax.psum(norm_part, ('dp', 'tp'))  14.3 us
    ppermute x2, waiting for transfers between devices, _bring_halves(): m_next.append(ppermute(m_next[-1], group_axis, gallery))  10.8 us
    ppermute x2, starting transfers between devices, shifted(): return lax.ppermute(array, axis, pairs)  6.95 us
    ppermute x2, waiting for transfers between devices, shifted(): return lax.ppermute(array, axis, pairs)  5.25 us
  transfers between devices with their start and end apart: 6, of which 5 were waited for; matrix products, arithmetic and copies ran while one was open for 11% of the time, Pallas kernels for 0%

profile of v1, /device:TPU:0, one launch (start us, length us, event | category | flops | bytes accessed | tf_op | source)
XLA Modules:
  0.0 200.5 jit_solution(3920284846306875344)
XLA Ops:
  7.2 0.8 copy.135
  8.1 0.1 reduce.1
  8.3 0.7 convert_divide_fusion
  9.0 0.3 multiply_cosine_fusion
  9.5 0.9 convert_bitcast_fusion.2
  10.4 0.7 fusion.45
  11.1 0.8 copy.142
  11.9 0.9 fusion.35
  12.9 0.7 pad_maximum_fusion
  13.5 5.5 %collective-permute-start = (bf16[2,128,2,128]{3,1,2,0:T(8,128)(2,1)}, bf16[2,128,2,128]{3,1,2,0:T(8,128)(2,1)}, u32[]{:S(2)}, u32[]{:S(2)}) collective-permute-start(bf16[2,128,2,128]{3,1,2,0:T(8,128)(2,1)} %pad_maximum_fusion), channel_id=1, source_target_pairs={{0,8},{8,16},{16,24},{1,9},{9,17},{17,25},{2,10},{10,18},{18,26},{... | collective-permute-start | bytes 393224 | tf_op jit(solution)/shard_map/ppermute | solution.py:38
  19.1 0.5 broadcast_compare_fusion
  19.7 0.7 copy.140
  20.4 0.1 convert_bitcast_fusion.1
  20.6 1.3 fusion.22
  21.9 1.6 copy.138
  23.5 0.4 copy.139
  23.9 0.4 copy.137
  24.4 1.0 fusion.40
  25.4 0.9 compare_and_fusion
  26.3 1.1 fusion.24
  27.3 0.3 fusion.51
  27.6 1.2 copy.164
  28.9 1.6 copy.168
  30.5 1.0 copy.169
  31.5 1.2 fusion.52
  32.8 0.4 fusion.29
  33.2 1.0 fusion.18
  34.2 1.0 convolution_bitcast_fusion.5
  35.2 0.4 convolution_bitcast_fusion.3
  35.6 1.2 fusion.3
  36.8 0.8 multiply_reduce_fusion
  37.7 1.5 fusion.12
  39.2 1.3 fusion.11
  40.5 0.3 fusion.19
  40.9 1.4 collective-permute-start.1
  42.3 0.3 fusion.15
  42.6 5.2 %collective-permute-done.1 = bf16[2,128,2,128]{3,1,2,0:T(8,128)(2,1)S(1)} collective-permute-done((bf16[2,128,2,128]{3,1,2,0:T(8,128)(2,1)S(1)}, bf16[2,128,2,128]{3,1,2,0:T(8,128)(2,1)S(1)}, u32[]{:S(2)}, u32[]{:S(2)}) %collective-permute-start.1) | collective-permute-done | bytes 131104 | tf_op jit(solution)/shard_map/ppermute | solution.py:38
  47.9 0.1 copy.167
  48.1 2.6 %convolution_bitcast_fusion = f32[4096,256]{0,1:T(8,128)} fusion(bf16[128,256]{0,1:T(8,128)(2,1)S(1)} %bitcast.172, bf16[128,4096]{0,1:T(8,128)(2,1)S(1)} %bitcast.170), kind=kOutput, calls=%fused_computation | convolution fusion | flops 268435456 | bytes 5308416 | tf_op jit(solution)/shard_map/dot_general | solution.py:208
  50.8 1.2 copy-done.10
  51.9 1.3 copy.166
  53.3 1.3 copy.170
  54.6 2.6 %copy.172 = f32[1024,256]{0,1:T(8,128)} copy(f32[1024,256]{1,0:T(8,128)} %param.19) | data formatting | bytes 2097152 | tf_op args[8]
  57.2 0.3 fusion.53
  57.5 1.2 fusion.6
  58.7 0.5 copy.157
  59.2 0.5 copy.156
  59.7 0.1 broadcast_multiply_fusion
  59.8 0.3 slice_bitcast_fusion
  60.2 88.6 %reduce-scatter.2.cloned.1.call-done = f32[256,256]{0,1:T(8,128)} async-done(((f32[4096,256]{0,1:T(8,128)}), f32[256,256]{0,1:T(8,128)}) %reduce-scatter.2.cloned.1.call-update) | async-done | bytes 262160 | tf_op jit(solution)/shard_map/reduce_scatter | solution.py:207
  148.8 1.1 fusion.25
  149.9 6.6 %collective-permute-done.2 = f32[256,256]{0,1:T(8,128)S(1)} collective-permute-done((f32[256,256]{0,1:T(8,128)}, f32[256,256]{0,1:T(8,128)S(1)}, u32[]{:S(2)}, u32[]{:S(2)}) %collective-permute-start.2) | collective-permute-done | bytes 262176 | tf_op jit(solution)/shard_map/ppermute | solution.py:27
  156.6 0.7 copy.174
  157.4 3.0 %collective-permute-start.4 = (f32[256,256]{0,1:T(8,128)S(1)}, f32[256,256]{0,1:T(8,128)S(1)}, u32[]{:S(2)}, u32[]{:S(2)}) collective-permute-start(f32[256,256]{0,1:T(8,128)S(1)} %copy-done.12), channel_id=1, source_target_pairs={{0,24},{8,0},{16,8},{24,16},{1,25},{9,1},{17,9},{25,17},{2,26},{10... | collective-permute-start | bytes 786440 | tf_op jit(solution)/shard_map/ppermute | solution.py:29
  160.4 4.3 %collective-permute-done.3 = f32[256,256]{0,1:T(8,128)S(1)} collective-permute-done((f32[256,256]{0,1:T(8,128)S(1)}, f32[256,256]{0,1:T(8,128)S(1)}, u32[]{:S(2)}, u32[]{:S(2)}) %collective-permute-start.3) | collective-permute-done | bytes 262176 | tf_op jit(solution)/shard_map/ppermute | solution.py:27
  164.8 1.9 collective-permute-done.4
  166.9 1.3 copy-done.6
  168.2 0.9 multiply_reduce_fusion.1
  169.1 0.7 copy.173
  169.8 14.3 %psum.7 = f32[]{:T(128)} all-reduce(f32[]{:T(128)} %multiply_reduce_fusion.1), channel_id=1, replica_groups=mesh['ctx'=4,'dp'=4,'tp'=2] {'dp','tp'}, use_global_device_ids=true, to_apply=%region_10.11 | all-reduce | flops 1 | bytes 8 | tf_op jit(solution)/shard_map/psum | solution.py:217
  184.9 3.5 %multiply_subtract_fusion = (f32[1024,256]{0,1:T(8,128)}, f32[1024,256]{0,1:T(8,128)}, f32[1024,256]{0,1:T(8,128)}) fusion(f32[1024,256]{0,1:T(8,128)S(1)} %copy-done.2, f32[]{:T(128)S(6)} %min_shard_map.3, f32[2048,256]{0,1:T(8,128)} %copy-done.6, s32[]{:T(128)S(6)} %select_n.36, f32[1024,256]{0,1:T(8,128)S(1)} %copy-done, f32[1024,256]{0,1:T(8,128)S(1)} %copy-done.1), kind=kLoop, calls=%fused_computation.48 | loop fusion | flops 4194304 | bytes 7340040 | tf_op jit(solution)/shard_map/sub | solution.py:81
  188.3 2.7 %copy.175 = f32[1024,256]{1,0:T(8,128)} copy(f32[1024,256]{0,1:T(8,128)} %get-tuple-element.35) | data formatting | bytes 2097152
  191.0 1.3 copy.176
  192.3 1.3 copy.177
  (75 shorter events, 1.1 us)
Async XLA Ops:
  7.2 13.2 %copy-start.18 = (bf16[1,128,16,128]{3,2,1,0:T(8,128)(2,1)S(1)}, bf16[1,128,16,128]{3,2,1,0:T(8,128)(2,1)}, u32[]{:S(2)}) copy-start(bf16[1,128,16,128]{3,2,1,0:T(8,128)(2,1)} %param.11) | copy-start | bytes 1572868
  7.2 141.6 %reduce-scatter.2.cloned.1.call-start = ((), (), s32[]{:S(2)}) async-start(), calls=%async_computation.1 | async-start | bytes 4456448 | tf_op jit(solution)/shard_map/reduce_scatter | solution.py:207
  13.5 18.0 %collective-permute-start = (bf16[2,128,2,128]{3,1,2,0:T(8,128)(2,1)}, bf16[2,128,2,128]{3,1,2,0:T(8,128)(2,1)}, u32[]{:S(2)}, u32[]{:S(2)}) collective-permute-start(bf16[2,128,2,128]{3,1,2,0:T(8,128)(2,1)} %pad_maximum_fusion), channel_id=1, source_target_pairs={{0,8},{8,16},{16,24},{1,9},{9,17},{17,25},{2,10},{10,18},{18,26},{... | collective-permute-start | bytes 393224 | tf_op jit(solution)/shard_map/ppermute | solution.py:38
  23.5 0.9 copy-start.17
  25.4 2.3 %copy-start.15 = (bf16[128,2,128,1]{2,0,3,1:T(8,128)(2,1)}, bf16[128,2,128,1]{2,0,3,1:T(8,128)(2,1)S(1)}, u32[]{:S(2)}) copy-start(bf16[128,2,128,1]{2,0,3,1:T(8,128)(2,1)S(1)} %fusion.40) | copy-start | bytes 196612
  26.2 1.4 copy-start.7
  31.5 1.6 copy-start.19
  34.2 1.0 copy-start.22
  37.7 1.5 copy-start.20
  39.2 1.6 copy-start.23
  40.5 2.1 %copy-start.8 = (bf16[2,8,128,128]{2,3,1,0:T(8,128)(2,1)}, bf16[2,8,128,128]{2,3,1,0:T(8,128)(2,1)S(1)}, u32[]{:S(2)}) copy-start(bf16[2,8,128,128]{2,3,1,0:T(8,128)(2,1)S(1)} %fusion.11) | copy-start | bytes 1572868
  40.5 7.4 %copy-start.21 = (f32[1,128,2,128]{3,1,2,0:T(8,128)S(1)}, f32[1,128,2,128]{3,1,2,0:T(8,128)}, u32[]{:S(2)}) copy-start(f32[1,128,2,128]{3,1,2,0:T(8,128)} %convolution_bitcast_fusion.5) | copy-start | bytes 393220
  40.5 7.5 %copy-start.3 = (bf16[128,4,4,256]{0,3,2,1:T(8,128)(2,1)S(1)}, bf16[128,4,4,256]{0,3,2,1:T(8,128)(2,1)}, u32[]{:S(2)}) copy-start(bf16[128,4,4,256]{0,3,2,1:T(8,128)(2,1)} %copy.169) | copy-start | bytes 3145732
  40.9 7.0 %collective-permute-start.1 = (bf16[2,128,2,128]{3,1,2,0:T(8,128)(2,1)S(1)}, bf16[2,128,2,128]{3,1,2,0:T(8,128)(2,1)S(1)}, u32[]{:S(2)}, u32[]{:S(2)}) collective-permute-start(bf16[2,128,2,128]{3,1,2,0:T(8,128)(2,1)S(1)} %pad_maximum_fusion.1), channel_id=1, source_target_pairs={{8,0},{16,8},{24,16},{9,1},{17,9},{25,17},{10,2},{18,10},{26,18},{... | collective-permute-start | bytes 393224 | tf_op jit(solution)/shard_map/ppermute | solution.py:38
  47.9 2.8 %copy-start.13 = (bf16[1,128,2,128]{3,1,2,0:T(8,128)(2,1)}, bf16[1,128,2,128]{3,1,2,0:T(8,128)(2,1)S(1)}, u32[]{:S(2)}) copy-start(bf16[1,128,2,128]{3,1,2,0:T(8,128)(2,1)S(1)} %slice.88) | copy-start | bytes 196612
  50.7 1.2 copy-start.10
  50.7 2.5 %copy-start.11 = (f32[1024,256]{1,0:T(8,128)S(1)}, f32[1024,256]{1,0:T(8,128)}, u32[]{:S(2)}) copy-start(f32[1024,256]{1,0:T(8,128)} %param.21) | copy-start | bytes 3145732
  53.3 3.9 %copy-start.16 = (bf16[128,2,128,1]{2,0,3,1:T(8,128)(2,1)S(1)}, bf16[128,2,128,1]{2,0,3,1:T(8,128)(2,1)}, u32[]{:S(2)}) copy-start(bf16[128,2,128,1]{2,0,3,1:T(8,128)(2,1)} %copy-done.15) | copy-start | bytes 196612
  54.6 2.9 %copy-start.9 = (bf16[2,8,128,128]{2,3,1,0:T(8,128)(2,1)S(1)}, bf16[2,8,128,128]{2,3,1,0:T(8,128)(2,1)}, u32[]{:S(2)}) copy-start(bf16[2,8,128,128]{2,3,1,0:T(8,128)(2,1)} %copy-done.8) | copy-start | bytes 1572868
  148.8 7.7 %collective-permute-start.2 = (f32[256,256]{0,1:T(8,128)}, f32[256,256]{0,1:T(8,128)S(1)}, u32[]{:S(2)}, u32[]{:S(2)}) collective-permute-start(f32[256,256]{0,1:T(8,128)} %reduce-scatter.2.cloned.1.call-done), channel_id=1, source_target_pairs={{0,8},{8,16},{16,24},{24,0},{1,9},{9,17},{17,25},{25,1},{2,10},{10... | collective-permute-start | bytes 786440 | tf_op jit(solution)/shard_map/ppermute | solution.py:27
  148.8 7.8 %copy-start.14 = (bf16[1,128,2,128]{3,1,2,0:T(8,128)(2,1)S(1)}, bf16[1,128,2,128]{3,1,2,0:T(8,128)(2,1)}, u32[]{:S(2)}) copy-start(bf16[1,128,2,128]{3,1,2,0:T(8,128)(2,1)} %copy-done.13) | copy-start | bytes 196612
  148.8 8.7 %copy-start.12 = (f32[256,256]{0,1:T(8,128)S(1)}, f32[256,256]{0,1:T(8,128)}, u32[]{:S(2)}) copy-start(f32[256,256]{0,1:T(8,128)} %reduce-scatter.2.cloned.1.call-done) | copy-start | bytes 786436
  156.5 8.2 %collective-permute-start.3 = (f32[256,256]{0,1:T(8,128)S(1)}, f32[256,256]{0,1:T(8,128)S(1)}, u32[]{:S(2)}, u32[]{:S(2)}) collective-permute-start(f32[256,256]{0,1:T(8,128)S(1)} %collective-permute-done.2), channel_id=1, source_target_pairs={{0,8},{8,16},{16,24},{24,0},{1,9},{9,17},{17,25},{25,1},{2,10},{10... | collective-permute-start | bytes 786440 | tf_op jit(solution)/shard_map/ppermute | solution.py:27
  157.4 9.2 %collective-permute-start.4 = (f32[256,256]{0,1:T(8,128)S(1)}, f32[256,256]{0,1:T(8,128)S(1)}, u32[]{:S(2)}, u32[]{:S(2)}) collective-permute-start(f32[256,256]{0,1:T(8,128)S(1)} %copy-done.12), channel_id=1, source_target_pairs={{0,24},{8,0},{16,8},{24,16},{1,25},{9,1},{17,9},{25,17},{2,26},{10... | collective-permute-start | bytes 786440 | tf_op jit(solution)/shard_map/ppermute | solution.py:29
  164.7 20.1 %copy-start = (f32[1024,256]{0,1:T(8,128)S(1)}, f32[1024,256]{0,1:T(8,128)}, u32[]{:S(2)}) copy-start(f32[1024,256]{0,1:T(8,128)} %copy.166) | copy-start | bytes 3145732
  164.8 20.1 %copy-start.1 = (f32[1024,256]{0,1:T(8,128)S(1)}, f32[1024,256]{0,1:T(8,128)}, u32[]{:S(2)}) copy-start(f32[1024,256]{0,1:T(8,128)} %copy.170) | copy-start | bytes 3145732
  164.8 20.1 %copy-start.2 = (f32[1024,256]{0,1:T(8,128)S(1)}, f32[1024,256]{0,1:T(8,128)}, u32[]{:S(2)}) copy-start(f32[1024,256]{0,1:T(8,128)} %copy.172) | copy-start | bytes 3145732
  166.8 1.4 copy-start.6
  188.3 2.7 %copy-start.5 = (f32[1024,256]{0,1:T(8,128)S(1)}, f32[1024,256]{0,1:T(8,128)}, u32[]{:S(2)}) copy-start(f32[1024,256]{0,1:T(8,128)} %get-tuple-element.36) | copy-start | bytes 3145732
  188.3 4.0 %copy-start.4 = (f32[1024,256]{0,1:T(8,128)S(1)}, f32[1024,256]{0,1:T(8,128)}, u32[]{:S(2)}) copy-start(f32[1024,256]{0,1:T(8,128)} %get-tuple-element.37) | copy-start | bytes 3145732
Sparse Core Ops, SparseCore 0:
  50.9 97.8 reduce-scatter.1
